TPU v7x, 32 devices: a whole 2x2x4 slice. The times are simulated.
32 devices in a mesh: groups: 2 (over y), seq: 4 (over z), head: 2 (over x), cfg: 2 (over core).
Axes of the slice: x: 2, y: 2, z: 4, core: 2. Of those that a mesh axis runs over, the one named last changes fastest.
Arguments:
- q_img: bfloat16 [2, 4096, 1536], P('cfg', ('groups', 'seq'), 'head'), parts along dimension 1
- k_img: bfloat16 [2, 4096, 1536], P('cfg', ('groups', 'seq'), 'head'), parts along dimension 1
- v_img: bfloat16 [2, 4096, 1536], P('cfg', ('groups', 'seq'), 'head'), parts along dimension 1, may hold values from -6 to 6
- text_keys: bfloat16 [2, 8, 333, 1536], P('cfg', 'groups', None, 'head'), parts along dimension 1
- text_values: bfloat16 [2, 8, 333, 1536], P('cfg', 'groups', None, 'head'), parts along dimension 1, may hold values from -6 to 6
- text_lengths: int32 [2, 8], P('cfg', 'groups'), parts along dimension 1, may hold values from 1 to 333, as said below
- img_lengths: int32 [8], P('groups'), parts along dimension 0, may hold values from 1 to 1024, 2048 in all
- out_weight: bfloat16 [1536, 2432], P(None, 'head'), may hold values from -0.15625 to 0.15625
Outputs:
- guided: bfloat16 [4096, 2432], P(('groups', 'seq'), ('head', 'cfg')), parts along dimension 0
There are 2 independent parts, one for each index of `groups`. A program takes and returns all parts, laid end to end along the dimension named above; an argument that names none is the same for every part. Nothing has to cross between parts.
Inputs may be any that keep to these rules, and one draw needn't show every extreme that they name: `img_lengths`: request r holds the image positions from the sum of the earlier lengths on; the lengths sum to 2048. text_lengths[b, r] of request r's 333 text slots are live in branch b, the first ones.
All inputs are finite; a program needn't handle non-finite values.
Results may differ from a plain program's by a relative error of at most 0.009.
Values may be sent and summed in bfloat16 or wider, within the bound.
No kernel may reach another device: no remote copies, remote signals or barrier semaphores. Data moves between devices by JAX's collectives and lax.ppermute only.
A program may use at most 128 MiB of HBM per device.

v0:
```python
import functools

import jax
import jax.numpy as jnp
from jax import lax
from jax.experimental import pallas as pl
from jax.experimental.pallas import tpu as pltpu
from jax.sharding import PartitionSpec as P

HDIM = 64


guidance = 4.0
score_scale = 0.125
neg_large = -1e30


def partner_2(x, axis, distance):
    return lax.ppermute(x, axis, [(i, i ^ 1 << distance) for i in range(lax.axis_size(axis))])


def seg_scalar(info_ref, pos, reqs):
    seg = jnp.int32(0)
    for r in range(reqs):
        seg = seg + jnp.where(pos >= info_ref[2 + r], 1, 0).astype(jnp.int32)
    return seg


def seg_vector(info_ref, pos, reqs):
    seg = jnp.zeros(pos.shape, jnp.int32)
    for r in range(reqs):
        seg = seg + (pos >= info_ref[2 + r]).astype(jnp.int32)
    return seg


def attn_kernel(info_ref, q_ref, k_ref, v_ref, *refs, kind, heads, reqs, tq, tk, total, first, last):
    if first:
        ins, outs = (), refs[:-3]
    else:
        ins, outs = refs[:3], refs[3:-3]
    m_sc, l_sc, a_sc = refs[-3:]
    qi = pl.program_id(0)
    b = pl.program_id(1)
    nb = pl.num_programs(1)
    width = heads * HDIM

    @pl.when(b == 0)
    def _():
        if first:
            m_sc[...] = jnp.full(m_sc.shape, neg_large, jnp.float32)
            l_sc[...] = jnp.zeros(l_sc.shape, jnp.float32)
            a_sc[...] = jnp.zeros(a_sc.shape, jnp.float32)
        else:
            m_sc[...] = ins[0][...]
            l_sc[...] = ins[1][...]
            a_sc[...] = ins[2][...]

    qpos0 = info_ref[0] + qi * tq
    qlo = seg_scalar(info_ref, qpos0, reqs)
    qhi = seg_scalar(info_ref, qpos0 + tq - 1, reqs)
    if kind == "text":
        active = (qlo <= b) & (b <= qhi)
    else:
        kpos0 = info_ref[1] + b * tk
        klo = seg_scalar(info_ref, kpos0, reqs)
        khi = seg_scalar(info_ref, kpos0 + tk - 1, reqs)
        active = (kpos0 >= 0) & (kpos0 < total) & (klo <= qhi) & (qlo <= khi)

    @pl.when(active)
    def _():
        qseg = seg_vector(info_ref, qpos0 + lax.broadcasted_iota(jnp.int32, (tq, 1), 0), reqs)
        col = lax.broadcasted_iota(jnp.int32, (1, tk), 1)
        if kind == "text":
            mask = (qseg == b) & (col < info_ref[2 + reqs + b])
        else:
            mask = qseg == seg_vector(info_ref, kpos0 + col, reqs)
        for g0 in range(0, width, 128):
            gw = min(128, width - g0)
            qg = q_ref[:, g0:g0 + gw]
            kg = k_ref[0, :, g0:g0 + gw]
            vg = v_ref[0, :, g0:g0 + gw]
            acc = a_sc[:, g0:g0 + gw]
            lane = lax.broadcasted_iota(jnp.int32, (1, gw), 1)
            lo = lane < HDIM
            parts = []
            for i in range(gw // HDIM):
                h = g0 // HDIM + i
                if gw == HDIM:
                    qh = qg
                else:
                    qh = jnp.where(lo if i == 0 else jnp.logical_not(lo), qg, jnp.zeros_like(qg))
                s = lax.dot_general(
                    qh, kg, (((1,), (1,)), ((), ())), preferred_element_type=jnp.float32
                ) * score_scale
                s = jnp.where(mask, s, neg_large)
                m_old = m_sc[h]
                m_new = jnp.maximum(m_old, jnp.max(s, axis=1, keepdims=True))
                alpha = jnp.exp(m_old - m_new)
                p = jnp.exp(s - m_new)
                l_sc[h] = alpha * l_sc[h] + jnp.sum(p, axis=1, keepdims=True)
                m_sc[h] = m_new
                pv = jnp.dot(p.astype(jnp.bfloat16), vg, preferred_element_type=jnp.float32)
                parts.append(alpha * acc + pv)
            new = parts[0] if len(parts) == 1 else jnp.where(lo, parts[0], parts[1])
            a_sc[:, g0:g0 + gw] = new

    @pl.when(b == nb - 1)
    def _():
        if last:
            for g0 in range(0, width, 128):
                gw = min(128, width - g0)
                h = g0 // HDIM
                if gw == HDIM:
                    den = l_sc[h]
                else:
                    lane = lax.broadcasted_iota(jnp.int32, (1, gw), 1)
                    den = jnp.where(lane < HDIM, l_sc[h], l_sc[h + 1])
                outs[0][:, g0:g0 + gw] = (a_sc[:, g0:g0 + gw] / den).astype(outs[0].dtype)
        else:
            outs[0][...] = m_sc[...]
            outs[1][...] = l_sc[...]
            outs[2][...] = a_sc[...]


def attend_chunk(info, queries, keys, values, state, *, kind, reqs, total, last):
    tok, width = queries.shape
    heads = width // HDIM
    nb, tk, _ = keys.shape
    tq = min(tok, 256)
    first = state is None
    kernel = functools.partial(
        attn_kernel, kind=kind, heads=heads, reqs=reqs, tq=tq, tk=tk, total=total, first=first, last=last
    )
    q_spec = pl.BlockSpec((tq, width), lambda qi, b, info: (qi, 0))
    kv_spec = pl.BlockSpec((1, tk, width), lambda qi, b, info: (b, 0, 0))
    ml_spec = pl.BlockSpec((heads, tq, 1), lambda qi, b, info: (0, qi, 0))
    in_specs = [q_spec, kv_spec, kv_spec]
    args = [queries, keys, values]
    if not first:
        in_specs += [ml_spec, ml_spec, q_spec]
        args += list(state)
    if last:
        out_shape = jax.ShapeDtypeStruct((tok, width), jnp.bfloat16)
        out_specs = q_spec
    else:
        out_shape = (
            jax.ShapeDtypeStruct((heads, tok, 1), jnp.float32),
            jax.ShapeDtypeStruct((heads, tok, 1), jnp.float32),
            jax.ShapeDtypeStruct((tok, width), jnp.float32),
        )
        out_specs = (ml_spec, ml_spec, q_spec)
    flops = 32 * 4 * tok * nb * tk * width * 2
    cost = pl.CostEstimate(
        flops=flops,
        transcendentals=tok * nb * tk * heads,
        bytes_accessed=2 * (tok * width * 2 + 2 * nb * tk * width * 2 + tok * width * 4),
    )
    return pl.pallas_call(
        kernel,
        out_shape=out_shape,
        grid_spec=pltpu.PrefetchScalarGridSpec(
            num_scalar_prefetch=1,
            grid=(tok // tq, nb),
            in_specs=in_specs,
            out_specs=out_specs,
            scratch_shapes=[
                pltpu.VMEM((heads, tq, 1), jnp.float32),
                pltpu.VMEM((heads, tq, 1), jnp.float32),
                pltpu.VMEM((tq, width), jnp.float32),
            ],
        ),
        compiler_params=pltpu.CompilerParams(dimension_semantics=("arbitrary", "arbitrary")),
        cost_estimate=cost,
    )(info, *args)


def local(q_img, k_img, v_img, text_keys, text_values, text_lengths, img_lengths, out_weight):
    tok_dev = q_img.shape[1]
    width = q_img.shape[2]
    reqs = text_keys.shape[1]
    text_slots = text_keys.shape[2]
    nseq = lax.axis_size("seq")
    me = lax.axis_index("seq")
    total = tok_dev * nseq
    longest = total // 2
    reach = min(nseq - 1, (longest + tok_dev - 2) // tok_dev)
    ends = jnp.cumsum(img_lengths).astype(jnp.int32)
    queries = q_img[0]

    def info_for(kstart):
        head = jnp.stack([me * tok_dev, kstart]).astype(jnp.int32)
        return jnp.concatenate([head, ends, text_lengths[0].astype(jnp.int32)])

    pad_to = -(-text_slots // 128) * 128
    pad = ((0, 0), (0, pad_to - text_slots), (0, 0))
    text_k = jnp.pad(text_keys[0], pad)
    text_v = jnp.pad(text_values[0], pad)
    tk = min(tok_dev, 256)

    def as_blocks(x):
        return x.reshape(tok_dev // tk, tk, width)

    common = dict(reqs=reqs, total=total)
    state = attend_chunk(info_for(0), queries, text_k, text_v, None, kind="text", last=False, **common)
    to_right = [(i, i + 1) for i in range(nseq - 1)]
    to_left = [(i + 1, i) for i in range(nseq - 1)]
    chunks = [(k_img[0], v_img[0], me * tok_dev)]
    left_k, left_v, right_k, right_v = k_img[0], v_img[0], k_img[0], v_img[0]
    for step in range(1, reach + 1):
        left_k = lax.ppermute(left_k, "seq", to_right)
        left_v = lax.ppermute(left_v, "seq", to_right)
        right_k = lax.ppermute(right_k, "seq", to_left)
        right_v = lax.ppermute(right_v, "seq", to_left)
        chunks.append((left_k, left_v, (me - step) * tok_dev))
        chunks.append((right_k, right_v, (me + step) * tok_dev))
    for index, (key_rows, val_rows, lower) in enumerate(chunks):
        state = attend_chunk(
            info_for(lower),
            queries,
            as_blocks(key_rows),
            as_blocks(val_rows),
            state,
            kind="image",
            last=index == len(chunks) - 1,
            **common,
        )
    attn = state
    own_cfg = lax.axis_index("cfg")
    cols = out_weight.shape[1]
    half = cols // 2
    mine_weight = jnp.where(own_cfg == 0, guidance, 1.0 - guidance)
    w_keep = lax.dynamic_slice_in_dim(out_weight, own_cfg * half, half, 1)
    w_out = lax.dynamic_slice_in_dim(out_weight, (1 - own_cfg) * half, half, 1)
    nhead = lax.axis_size("head")
    if nhead == 2:
        hx = lax.axis_index("head")
        other = partner_2(attn, "head", 0)

        def project(w):
            w_mine = lax.dynamic_slice_in_dim(w, hx * width, width, 0)
            w_other = lax.dynamic_slice_in_dim(w, (1 - hx) * width, width, 0)
            own = lax.optimization_barrier(jnp.dot(attn, w_mine, preferred_element_type=jnp.float32))
            return own + jnp.dot(other, w_other, preferred_element_type=jnp.float32)
    else:
        gathered = lax.all_gather(attn, "head", axis=1, tiled=True)

        def project(w):
            return jnp.dot(gathered, w, preferred_element_type=jnp.float32)

    outgoing = project(w_out)
    partner = partner_2(outgoing.astype(jnp.bfloat16), "cfg", 0).astype(outgoing.dtype)
    keep = project(w_keep)
    guided = mine_weight * keep + (1.0 - mine_weight) * partner
    return guided.astype(jnp.bfloat16)


def solution(mesh):
    placed = (
        P("cfg", ("groups", "seq"), "head"),
        P("cfg", ("groups", "seq"), "head"),
        P("cfg", ("groups", "seq"), "head"),
        P("cfg", "groups", None, "head"),
        P("cfg", "groups", None, "head"),
        P("cfg", "groups"),
        P("groups"),
        P(None, "head"),
    )
    return jax.shard_map(
        local,
        mesh=mesh,
        in_specs=placed,
        out_specs=P(("groups", "seq"), ("head", "cfg")),
        check_vma=False,
    )
```

profile of v0, /device:TPU:15, one launch (start us, length us, event | category | flops | bytes accessed | tf_op | source)
XLA Modules:
  0.0 189.5 jit_solution(17358143590286647227)
XLA Ops:
  0.0 3.2 %collective-permute-start.4 = (bf16[512,768]{1,0:T(8,128)(2,1)}, bf16[512,768]{1,0:T(8,128)(2,1)}, u32[]{:S(2)}, u32[]{:S(2)}) collective-permute-start(bf16[512,768]{1,0:T(8,128)(2,1)} %bitcast.39), channel_id=1, source_target_pairs={{0,4},{4,8},{8,12},{1,5},{5,9},{9,13},{2,6},{6,10},{10,14},{3,7},{... | collective-permute-start | bytes 2359304 | tf_op jit(solution)/shard_map/ppermute | solution.py:210
  3.2 3.0 %collective-permute-start = (bf16[512,768]{1,0:T(8,128)(2,1)}, bf16[512,768]{1,0:T(8,128)(2,1)}, u32[]{:S(2)}, u32[]{:S(2)}) collective-permute-start(bf16[512,768]{1,0:T(8,128)(2,1)} %bitcast.40), channel_id=1, source_target_pairs={{4,0},{8,4},{12,8},{5,1},{9,5},{13,9},{6,2},{10,6},{14,10},{7,3},{... | collective-permute-start | bytes 2359304 | tf_op jit(solution)/shard_map/ppermute | solution.py:212
  6.2 2.3 %collective-permute-start.6 = (bf16[512,768]{1,0:T(8,128)(2,1)}, bf16[512,768]{1,0:T(8,128)(2,1)}, u32[]{:S(2)}, u32[]{:S(2)}) collective-permute-start(bf16[512,768]{1,0:T(8,128)(2,1)} %bitcast.42), channel_id=1, source_target_pairs={{0,4},{4,8},{8,12},{1,5},{5,9},{9,13},{2,6},{6,10},{10,14},{3,7},{... | collective-permute-start | bytes 2359304 | tf_op jit(solution)/shard_map/ppermute | solution.py:211
  8.5 3.8 %collective-permute-start.2 = (bf16[512,768]{1,0:T(8,128)(2,1)}, bf16[512,768]{1,0:T(8,128)(2,1)}, u32[]{:S(2)}, u32[]{:S(2)}) collective-permute-start(bf16[512,768]{1,0:T(8,128)(2,1)} %bitcast.43), channel_id=1, source_target_pairs={{4,0},{8,4},{12,8},{5,1},{9,5},{13,9},{6,2},{10,6},{14,10},{7,3},{... | collective-permute-start | bytes 2359304 | tf_op jit(solution)/shard_map/ppermute | solution.py:213
  12.4 0.0 copy-start.1
  12.4 2.0 %copy.14 = bf16[1,4,333,768]{3,2,1,0:T(8,128)(2,1)S(1)} copy(bf16[1,4,333,768]{3,1,2,0:T(4,128)(2,1)} %param.11) | data formatting | bytes 4091904 | tf_op args[3]
  14.4 0.2 copy-done.1
  14.6 0.3 copy.13
  14.8 1.6 pad.7.k_ref
  16.4 0.0 copy-start.10
  16.4 0.0 copy-start.2
  16.4 1.6 pad.8.v_ref
  18.0 0.0 copy-done.10
  18.0 0.2 reduce-window.9
  18.2 0.0 copy-start.4
  18.2 0.0 copy-done.2
  18.2 0.6 add_add_fusion.4
  18.8 0.6 add_add_fusion.5
  19.4 23.5 %shard_map.82 = (f32[12,512,1]{2,1,0:T(8,128)}, f32[12,512,1]{2,1,0:T(8,128)}, f32[512,768]{1,0:T(8,128)}) custom-call(s32[10]{0:T(128)} %get-tuple-element.35.info_ref, bf16[512,768]{1,0:T(8,128)(2,1)} %bitcast.45, bf16[4,384,768]{2,1,0:T(8,128)(2,1)} %pad.7.k_ref, bf16[4,384,768]{2,1,0:T(8,128)(2,1)} %pad.8.v_ref), custom_call_target="tpu_custom_call" | custom-call | flops 154618822656 | bytes 14155776 | tf_op jit(solution)/shard_map/pallas_call | solution.py:158
  42.9 0.0 copy-done.4
  42.9 0.0 copy-start.3
  42.9 0.0 copy-start.5
  42.9 23.5 %shard_map.83 = (f32[12,512,1]{2,1,0:T(8,128)}, f32[12,512,1]{2,1,0:T(8,128)}, f32[512,768]{1,0:T(8,128)}) custom-call(s32[10]{0:T(128)} %get-tuple-element.37.info_ref, bf16[512,768]{1,0:T(8,128)(2,1)} %bitcast.46, bf16[2,256,768]{2,1,0:T(8,128)(2,1)} %bitcast.41, bf16[2,256,768]{2,1,0:T(8,128)(2,1)} %bitcast.44, f32[12,512,1]{2,1,0:T(8,128)} %get-tuple-element.20.refs_0_, ...), custom_call_target="tpu_custom_call" | custom-call | flops 51539607552 | bytes 7864320 | tf_op jit(solution)/shard_map/pallas_call | solution.py:158
  66.4 0.0 copy-done.3
  66.4 0.0 copy-done.5
  66.4 0.6 add_add_fusion.3
  67.0 0.0 collective-permute-done.4
  67.1 0.0 collective-permute-done.6
  67.1 23.6 %shard_map.84 = (f32[12,512,1]{2,1,0:T(8,128)}, f32[12,512,1]{2,1,0:T(8,128)}, f32[512,768]{1,0:T(8,128)}) custom-call(s32[10]{0:T(128)} %get-tuple-element.39.info_ref, bf16[512,768]{1,0:T(8,128)(2,1)} %bitcast.47, bf16[2,256,768]{2,1,0:T(8,128)(2,1)} %bitcast.17.k_ref, bf16[2,256,768]{2,1,0:T(8,128)(2,1)} %bitcast.18.v_ref, ...), custom_call_target="tpu_custom_call" | custom-call | flops 51539607552 | bytes 7864320 | tf_op jit(solution)/shard_map/pallas_call | solution.py:158
  90.7 1.9 %collective-permute-start.5 = (bf16[512,768]{1,0:T(8,128)(2,1)}, bf16[512,768]{1,0:T(8,128)(2,1)S(1)}, u32[]{:S(2)}, u32[]{:S(2)}) collective-permute-start(bf16[512,768]{1,0:T(8,128)(2,1)} %collective-permute-done.4), channel_id=1, source_target_pairs={{0,4},{4,8},{8,12},{1,5},{5,9},{9,13},{2,6},{6,10},{10,14},{3,7},{... | collective-permute-start | bytes 2359304 | tf_op jit(solution)/shard_map/ppermute | solution.py:210
  92.6 1.9 %collective-permute-start.7 = (bf16[512,768]{1,0:T(8,128)(2,1)}, bf16[512,768]{1,0:T(8,128)(2,1)S(1)}, u32[]{:S(2)}, u32[]{:S(2)}) collective-permute-start(bf16[512,768]{1,0:T(8,128)(2,1)} %collective-permute-done.6), channel_id=1, source_target_pairs={{0,4},{4,8},{8,12},{1,5},{5,9},{9,13},{2,6},{6,10},{10,14},{3,7},{... | collective-permute-start | bytes 2359304 | tf_op jit(solution)/shard_map/ppermute | solution.py:211
  94.5 0.0 collective-permute-done
  94.5 0.0 collective-permute-done.2
  94.5 9.9 %shard_map.85 = (f32[12,512,1]{2,1,0:T(8,128)}, f32[12,512,1]{2,1,0:T(8,128)}, f32[512,768]{1,0:T(8,128)}) custom-call(s32[10]{0:T(128)} %get-tuple-element.38.info_ref, bf16[512,768]{1,0:T(8,128)(2,1)} %bitcast.48, bf16[2,256,768]{2,1,0:T(8,128)(2,1)} %bitcast.14.k_ref, bf16[2,256,768]{2,1,0:T(8,128)(2,1)} %bitcast.15.v_ref, ...), custom_call_target="tpu_custom_call" | custom-call | flops 51539607552 | bytes 7864320 | tf_op jit(solution)/shard_map/pallas_call | solution.py:158
  104.5 16.9 %collective-permute-start.1 = (bf16[512,768]{1,0:T(8,128)(2,1)}, bf16[512,768]{1,0:T(8,128)(2,1)S(1)}, u32[]{:S(2)}, u32[]{:S(2)}) collective-permute-start(bf16[512,768]{1,0:T(8,128)(2,1)} %collective-permute-done), channel_id=1, source_target_pairs={{4,0},{8,4},{12,8},{5,1},{9,5},{13,9},{6,2},{10,6},{14,10},{7,3},{... | collective-permute-start | bytes 2359304 | tf_op jit(solution)/shard_map/ppermute | solution.py:212
  121.4 1.9 %collective-permute-start.3 = (bf16[512,768]{1,0:T(8,128)(2,1)}, bf16[512,768]{1,0:T(8,128)(2,1)S(1)}, u32[]{:S(2)}, u32[]{:S(2)}) collective-permute-start(bf16[512,768]{1,0:T(8,128)(2,1)} %collective-permute-done.2), channel_id=1, source_target_pairs={{4,0},{8,4},{12,8},{5,1},{9,5},{13,9},{6,2},{10,6},{14,10},{7,3},{... | collective-permute-start | bytes 2359304 | tf_op jit(solution)/shard_map/ppermute | solution.py:213
  123.3 0.0 collective-permute-done.5
  123.4 0.0 copy-start.6
  123.4 3.5 %collective-permute-done.7 = bf16[512,768]{1,0:T(8,128)(2,1)S(1)} collective-permute-done((bf16[512,768]{1,0:T(8,128)(2,1)}, bf16[512,768]{1,0:T(8,128)(2,1)S(1)}, u32[]{:S(2)}, u32[]{:S(2)}) %collective-permute-start.7) | collective-permute-done | bytes 786464 | tf_op jit(solution)/shard_map/ppermute | solution.py:211
  126.9 0.0 copy-start.7
  126.9 0.0 copy-done.6
  126.9 0.9 copy-done.7
  127.7 10.1 %shard_map.86 = (f32[12,512,1]{2,1,0:T(8,128)}, f32[12,512,1]{2,1,0:T(8,128)}, f32[512,768]{1,0:T(8,128)}) custom-call(s32[10]{0:T(128)} %get-tuple-element.36.info_ref, bf16[512,768]{1,0:T(8,128)(2,1)} %bitcast.49, bf16[2,256,768]{2,1,0:T(8,128)(2,1)} %bitcast.51, bf16[2,256,768]{2,1,0:T(8,128)(2,1)} %bitcast.52, f32[12,512,1]{2,1,0:T(8,128)} %get-tuple-element.29.refs_0_, ...), custom_call_target="tpu_custom_call" | custom-call | flops 51539607552 | bytes 7864320 | tf_op jit(solution)/shard_map/pallas_call | solution.py:158
  137.8 0.0 collective-permute-done.1
  137.8 0.0 copy-start.8
  137.8 15.5 %collective-permute-done.3 = bf16[512,768]{1,0:T(8,128)(2,1)S(1)} collective-permute-done((bf16[512,768]{1,0:T(8,128)(2,1)}, bf16[512,768]{1,0:T(8,128)(2,1)S(1)}, u32[]{:S(2)}, u32[]{:S(2)}) %collective-permute-start.3) | collective-permute-done | bytes 786464 | tf_op jit(solution)/shard_map/ppermute | solution.py:213
  153.3 0.0 copy-start.9
  153.3 0.0 copy-done.8
  153.3 1.0 copy-done.9
  154.3 7.6 %shard_map.87 = bf16[512,768]{1,0:T(8,128)(2,1)} custom-call(s32[10]{0:T(128)} %get-tuple-element.40.info_ref, bf16[512,768]{1,0:T(8,128)(2,1)} %bitcast.50, bf16[2,256,768]{2,1,0:T(8,128)(2,1)} %bitcast.53, bf16[2,256,768]{2,1,0:T(8,128)(2,1)} %bitcast.54, f32[12,512,1]{2,1,0:T(8,128)} %get-tuple-element.32.refs_0_, ...), custom_call_target="tpu_custom_call" | custom-call | flops 51539607552 | bytes 7864320 | tf_op jit(solution)/shard_map/pallas_call | solution.py:158
  161.9 0.2 collective-permute-start.8
  162.2 2.1 %fusion.2 = f32[512,608]{0,1:T(8,128)S(1)} fusion(bf16[512,768]{1,0:T(8,128)(2,1)} %shard_map.87, bf16[1536,1216]{0,1:T(8,128)(2,1)} %param.15, s32[]{:T(128)S(6)} %select_n.28, s32[]{:T(128)S(6)} %select_n.34), kind=kOutput, calls=%fused_computation.6 | convolution fusion | flops 478150656 | bytes 2965512 | tf_op jit(solution)/shard_map/dot_general | solution.py:242
  164.3 13.9 %collective-permute-done.8 = bf16[512,768]{1,0:T(8,128)(2,1)S(1)} collective-permute-done((bf16[512,768]{1,0:T(8,128)(2,1)}, bf16[512,768]{1,0:T(8,128)(2,1)S(1)}, u32[]{:S(2)}, u32[]{:S(2)}) %collective-permute-start.8) | collective-permute-done | bytes 786464 | tf_op jit(solution)/shard_map/ppermute | solution.py:19
  178.2 1.9 %fusion = f32[512,608]{0,1:T(8,128)S(1)} fusion(bf16[512,768]{1,0:T(8,128)(2,1)S(1)} %collective-permute-done.8, bf16[1536,1216]{0,1:T(8,128)(2,1)} %param.15, s32[]{:T(128)S(6)} %select_n.32, s32[]{:T(128)S(6)} %select_n.34), kind=kOutput, calls=%fused_computation.4 | convolution fusion | flops 478150656 | bytes 2965512 | tf_op jit(solution)/shard_map/dot_general | solution.py:243
  180.1 0.0 copy-start
  180.1 0.3 add_convert_fusion.1
  180.4 4.0 %collective-permute-start.9 = (bf16[512,608]{0,1:T(8,128)(2,1)S(1)}, bf16[512,608]{0,1:T(8,128)(2,1)S(1)}, u32[]{:S(2)}, u32[]{:S(2)}) collective-permute-start(bf16[512,608]{0,1:T(8,128)(2,1)S(1)} %add_convert_fusion.1), channel_id=1, source_target_pairs={{0,1},{1,0},{2,3},{3,2},{4,5},{5,4},{6,7},{7,6},{8,9},{9,8},{10,11... | collective-permute-start | bytes 1867784 | tf_op jit(solution)/shard_map/ppermute | solution.py:19
  184.4 0.0 copy-done
  184.4 1.9 fusion.6
  186.3 1.9 %fusion.4 = f32[512,608]{0,1:T(8,128)S(1)} fusion(bf16[512,768]{1,0:T(8,128)(2,1)S(1)} %collective-permute-done.8, bf16[1536,1216]{0,1:T(8,128)(2,1)} %param.15, s32[]{:T(128)S(6)} %select_n.32, s32[]{:T(128)S(6)} %select_n.30), kind=kOutput, calls=%fused_computation.8 | convolution fusion | flops 478150656 | bytes 2965512 | tf_op jit(solution)/shard_map/dot_general | solution.py:243
  188.3 0.0 collective-permute-done.9
  188.3 1.2 add_convert_fusion
Async XLA Ops:
  0.0 67.1 %collective-permute-start.4 = (bf16[512,768]{1,0:T(8,128)(2,1)}, bf16[512,768]{1,0:T(8,128)(2,1)}, u32[]{:S(2)}, u32[]{:S(2)}) collective-permute-start(bf16[512,768]{1,0:T(8,128)(2,1)} %bitcast.39), channel_id=1, source_target_pairs={{0,4},{4,8},{8,12},{1,5},{5,9},{9,13},{2,6},{6,10},{10,14},{3,7},{... | collective-permute-start | bytes 2359304 | tf_op jit(solution)/shard_map/ppermute | solution.py:210
  3.2 91.3 %collective-permute-start = (bf16[512,768]{1,0:T(8,128)(2,1)}, bf16[512,768]{1,0:T(8,128)(2,1)}, u32[]{:S(2)}, u32[]{:S(2)}) collective-permute-start(bf16[512,768]{1,0:T(8,128)(2,1)} %bitcast.40), channel_id=1, source_target_pairs={{4,0},{8,4},{12,8},{5,1},{9,5},{13,9},{6,2},{10,6},{14,10},{7,3},{... | collective-permute-start | bytes 2359304 | tf_op jit(solution)/shard_map/ppermute | solution.py:212
  6.2 60.9 %collective-permute-start.6 = (bf16[512,768]{1,0:T(8,128)(2,1)}, bf16[512,768]{1,0:T(8,128)(2,1)}, u32[]{:S(2)}, u32[]{:S(2)}) collective-permute-start(bf16[512,768]{1,0:T(8,128)(2,1)} %bitcast.42), channel_id=1, source_target_pairs={{0,4},{4,8},{8,12},{1,5},{5,9},{9,13},{2,6},{6,10},{10,14},{3,7},{... | collective-permute-start | bytes 2359304 | tf_op jit(solution)/shard_map/ppermute | solution.py:211
  8.5 86.0 %collective-permute-start.2 = (bf16[512,768]{1,0:T(8,128)(2,1)}, bf16[512,768]{1,0:T(8,128)(2,1)}, u32[]{:S(2)}, u32[]{:S(2)}) collective-permute-start(bf16[512,768]{1,0:T(8,128)(2,1)} %bitcast.43), channel_id=1, source_target_pairs={{4,0},{8,4},{12,8},{5,1},{9,5},{13,9},{6,2},{10,6},{14,10},{7,3},{... | collective-permute-start | bytes 2359304 | tf_op jit(solution)/shard_map/ppermute | solution.py:213
  12.4 2.2 %copy-start.1 = (bf16[1,4,333,768]{3,1,2,0:T(4,128)(2,1)S(1)}, bf16[1,4,333,768]{3,1,2,0:T(4,128)(2,1)}, u32[]{:S(2)}) copy-start(bf16[1,4,333,768]{3,1,2,0:T(4,128)(2,1)} %param.12) | copy-start | bytes 6137860
  16.4 1.6 copy-start.10
  16.4 1.8 copy-start.2
  18.2 24.7 %copy-start.4 = (s32[4,1]{0,1:T(1,128)}, s32[4,1]{0,1:T(1,128)S(1)}, u32[]{:S(2)}) copy-start(s32[4,1]{0,1:T(1,128)S(1)} %reduce-window.9) | copy-start | bytes 52
  42.9 23.5 %copy-start.3 = (s32[1,4]{1,0:T(1,128)S(1)}, s32[1,4]{1,0:T(1,128)}, u32[]{:S(2)}) copy-start(s32[1,4]{1,0:T(1,128)} %param.13) | copy-start | bytes 52
  42.9 23.5 %copy-start.5 = (s32[4,1]{0,1:T(1,128)S(1)}, s32[4,1]{0,1:T(1,128)}, u32[]{:S(2)}) copy-start(s32[4,1]{0,1:T(1,128)} %copy-done.4) | copy-start | bytes 52
  90.7 32.7 %collective-permute-start.5 = (bf16[512,768]{1,0:T(8,128)(2,1)}, bf16[512,768]{1,0:T(8,128)(2,1)S(1)}, u32[]{:S(2)}, u32[]{:S(2)}) collective-permute-start(bf16[512,768]{1,0:T(8,128)(2,1)} %collective-permute-done.4), channel_id=1, source_target_pairs={{0,4},{4,8},{8,12},{1,5},{5,9},{9,13},{2,6},{6,10},{10,14},{3,7},{... | collective-permute-start | bytes 2359304 | tf_op jit(solution)/shard_map/ppermute | solution.py:210
  92.6 34.3 %collective-permute-start.7 = (bf16[512,768]{1,0:T(8,128)(2,1)}, bf16[512,768]{1,0:T(8,128)(2,1)S(1)}, u32[]{:S(2)}, u32[]{:S(2)}) collective-permute-start(bf16[512,768]{1,0:T(8,128)(2,1)} %collective-permute-done.6), channel_id=1, source_target_pairs={{0,4},{4,8},{8,12},{1,5},{5,9},{9,13},{2,6},{6,10},{10,14},{3,7},{... | collective-permute-start | bytes 2359304 | tf_op jit(solution)/shard_map/ppermute | solution.py:211
  104.5 33.4 %collective-permute-start.1 = (bf16[512,768]{1,0:T(8,128)(2,1)}, bf16[512,768]{1,0:T(8,128)(2,1)S(1)}, u32[]{:S(2)}, u32[]{:S(2)}) collective-permute-start(bf16[512,768]{1,0:T(8,128)(2,1)} %collective-permute-done), channel_id=1, source_target_pairs={{4,0},{8,4},{12,8},{5,1},{9,5},{13,9},{6,2},{10,6},{14,10},{7,3},{... | collective-permute-start | bytes 2359304 | tf_op jit(solution)/shard_map/ppermute | solution.py:212
  121.4 31.9 %collective-permute-start.3 = (bf16[512,768]{1,0:T(8,128)(2,1)}, bf16[512,768]{1,0:T(8,128)(2,1)S(1)}, u32[]{:S(2)}, u32[]{:S(2)}) collective-permute-start(bf16[512,768]{1,0:T(8,128)(2,1)} %collective-permute-done.2), channel_id=1, source_target_pairs={{4,0},{8,4},{12,8},{5,1},{9,5},{13,9},{6,2},{10,6},{14,10},{7,3},{... | collective-permute-start | bytes 2359304 | tf_op jit(solution)/shard_map/ppermute | solution.py:213
  123.4 3.5 %copy-start.6 = (bf16[512,768]{1,0:T(8,128)(2,1)}, bf16[512,768]{1,0:T(8,128)(2,1)S(1)}, u32[]{:S(2)}) copy-start(bf16[512,768]{1,0:T(8,128)(2,1)S(1)} %collective-permute-done.5) | copy-start | bytes 2359300
  126.9 0.9 copy-start.7
  137.8 15.5 %copy-start.8 = (bf16[512,768]{1,0:T(8,128)(2,1)}, bf16[512,768]{1,0:T(8,128)(2,1)S(1)}, u32[]{:S(2)}) copy-start(bf16[512,768]{1,0:T(8,128)(2,1)S(1)} %collective-permute-done.1) | copy-start | bytes 2359300
  153.3 1.0 copy-start.9
  161.9 16.2 %collective-permute-start.8 = (bf16[512,768]{1,0:T(8,128)(2,1)}, bf16[512,768]{1,0:T(8,128)(2,1)S(1)}, u32[]{:S(2)}, u32[]{:S(2)}) collective-permute-start(bf16[512,768]{1,0:T(8,128)(2,1)} %shard_map.87), channel_id=1, source_target_pairs={{0,2},{2,0},{1,3},{3,1},{4,6},{6,4},{5,7},{7,5},{8,10},{10,8},{9,1... | collective-permute-start | bytes 2359304 | tf_op jit(solution)/shard_map/ppermute | solution.py:19
  180.1 4.3 %copy-start = (bf16[512,768]{1,0:T(8,128)(2,1)S(1)}, bf16[512,768]{1,0:T(8,128)(2,1)}, u32[]{:S(2)}) copy-start(bf16[512,768]{1,0:T(8,128)(2,1)} %shard_map.87) | copy-start | bytes 2359300
  180.4 7.8 %collective-permute-start.9 = (bf16[512,608]{0,1:T(8,128)(2,1)S(1)}, bf16[512,608]{0,1:T(8,128)(2,1)S(1)}, u32[]{:S(2)}, u32[]{:S(2)}) collective-permute-start(bf16[512,608]{0,1:T(8,128)(2,1)S(1)} %add_convert_fusion.1), channel_id=1, source_target_pairs={{0,1},{1,0},{2,3},{3,2},{4,5},{5,4},{6,7},{7,6},{8,9},{9,8},{10,11... | collective-permute-start | bytes 1867784 | tf_op jit(solution)/shard_map/ppermute | solution.py:19
where the time goes:
time: 190 us
  Pallas kernels  98.3 us (52%)
  starting transfers between devices  39.2 us (21%)
  waiting for transfers between devices  32.9 us (17%)
  matrix products  7.89 us (4%)
  local copies, waits for them, and re-layouts  7.48 us (4%)
  other arithmetic  3.57 us (2%)
    pallas_call x6, Pallas kernels, attend_chunk(): pl.pallas_call(kernel, out_shape=out_shape, grid_spec=pltpu.PrefetchScala...  98.3 us
    ppermute x2, starting transfers between devices, local(): right_k = lax.ppermute(right_k, 'seq', to_left)  19.9 us
    ppermute x2, waiting for transfers between devices, local(): right_v = lax.ppermute(right_v, 'seq', to_left)  15.5 us
    ppermute x2, waiting for transfers between devices, partner_2(): lax.ppermute(x, axis, [(i, i ^ 1 << distance) for i in range(lax.axis_siz...  13.9 us
    ppermute x2, starting transfers between devices, local(): right_v = lax.ppermute(right_v, 'seq', to_left)  5.76 us
    ppermute x2, starting transfers between devices, local(): left_k = lax.ppermute(left_k, 'seq', to_right)  5.1 us
    unnamed x24, local copies, waits for them, and re-layouts  4.29 us
    ppermute x2, starting transfers between devices, local(): left_v = lax.ppermute(left_v, 'seq', to_right)  4.22 us
  transfers between devices with their start and end apart: 10, of which 3 were waited for; matrix products, arithmetic and copies ran while one was open for 7% of the time, Pallas kernels for 48%

commit v1 on v0

--- a/solution.py
+++ b/solution.py
@@ -202,17 +202,18 @@
 
     common = dict(reqs=reqs, total=total)
     state = attend_chunk(info_for(0), queries, text_k, text_v, None, kind="text", last=False, **common)
-    to_right = [(i, i + 1) for i in range(nseq - 1)]
-    to_left = [(i + 1, i) for i in range(nseq - 1)]
     chunks = [(k_img[0], v_img[0], me * tok_dev)]
-    left_k, left_v, right_k, right_v = k_img[0], v_img[0], k_img[0], v_img[0]
     for step in range(1, reach + 1):
-        left_k = lax.ppermute(left_k, "seq", to_right)
-        left_v = lax.ppermute(left_v, "seq", to_right)
-        right_k = lax.ppermute(right_k, "seq", to_left)
-        right_v = lax.ppermute(right_v, "seq", to_left)
-        chunks.append((left_k, left_v, (me - step) * tok_dev))
-        chunks.append((right_k, right_v, (me + step) * tok_dev))
+        to_right = [(i, i + step) for i in range(nseq - step)]
+        to_left = [(i + step, i) for i in range(nseq - step)]
+        for pairs, sign in ((to_right, -1), (to_left, 1)):
+            chunks.append(
+                (
+                    lax.ppermute(k_img[0], "seq", pairs),
+                    lax.ppermute(v_img[0], "seq", pairs),
+                    (me + sign * step) * tok_dev,
+                )
+            )
     for index, (key_rows, val_rows, lower) in enumerate(chunks):
         state = attend_chunk(
             info_for(lower),

time: 190 us -> 181 us (0.953)
  the two profiles are of different devices: /device:TPU:15 before, /device:TPU:0 now
where the time goes in v1:
time: 181 us; the launch traced here: 182 us
  Pallas kernels  93.3 us (52%)
  waiting for transfers between devices  44.2 us (24%)
  starting transfers between devices  24.6 us (14%)
  local copies, waits for them, and re-layouts  8.19 us (5%)
  matrix products  7.89 us (4%)
  other arithmetic  3.65 us (2%)
    pallas_call x6, Pallas kernels, attend_chunk(): pl.pallas_call(kernel, out_shape=out_shape, grid_spec=pltpu.PrefetchScala...  93.3 us
    ppermute x4, waiting for transfers between devices, local(): lax.ppermute(k_img[0], 'seq', pairs)  15.1 us
    ppermute x4, waiting for transfers between devices, local(): lax.ppermute(v_img[0], 'seq', pairs)  14.9 us
    ppermute x2, waiting for transfers between devices, partner_2(): lax.ppermute(x, axis, [(i, i ^ 1 << distance) for i in range(lax.axis_siz...  14.2 us
    ppermute x4, starting transfers between devices, local(): lax.ppermute(k_img[0], 'seq', pairs)  13.7 us
    ppermute x4, starting transfers between devices, local(): lax.ppermute(v_img[0], 'seq', pairs)  9.35 us
    unnamed x22, local copies, waits for them, and re-layouts  5.01 us
    dot_general x2, matrix products, project(): jnp.dot(attn, w_mine, preferred_element_type=jnp.float32)  4.11 us
  transfers between devices with their start and end apart: 10, of which 3 were waited for; matrix products, arithmetic and copies ran while one was open for 7% of the time, Pallas kernels for 47%

profile of v1, /device:TPU:0, one launch (start us, length us, event | category | flops | bytes accessed | tf_op | source)
XLA Modules:
  0.0 182.0 jit_solution(2805390463567810524)
XLA Ops:
  0.0 5.8 %collective-permute-start.6 = (bf16[512,768]{1,0:T(8,128)(2,1)}, bf16[512,768]{1,0:T(8,128)(2,1)}, u32[]{:S(2)}, u32[]{:S(2)}) collective-permute-start(bf16[512,768]{1,0:T(8,128)(2,1)} %bitcast.6), channel_id=1, source_target_pairs={{0,4},{4,8},{8,12},{1,5},{5,9},{9,13},{2,6},{6,10},{10,14},{3,7},{... | collective-permute-start | bytes 2359304 | tf_op jit(solution)/shard_map/ppermute | solution.py:212
  5.8 1.3 collective-permute-start.4
  7.1 5.4 %collective-permute-start.7 = (bf16[512,768]{1,0:T(8,128)(2,1)}, bf16[512,768]{1,0:T(8,128)(2,1)}, u32[]{:S(2)}, u32[]{:S(2)}) collective-permute-start(bf16[512,768]{1,0:T(8,128)(2,1)} %bitcast.39), channel_id=1, source_target_pairs={{0,4},{4,8},{8,12},{1,5},{5,9},{9,13},{2,6},{6,10},{10,14},{3,7},{... | collective-permute-start | bytes 2359304 | tf_op jit(solution)/shard_map/ppermute | solution.py:213
  12.5 1.3 collective-permute-start.5
  13.8 5.2 %collective-permute-start.2 = (bf16[512,768]{1,0:T(8,128)(2,1)}, bf16[512,768]{1,0:T(8,128)(2,1)}, u32[]{:S(2)}, u32[]{:S(2)}) collective-permute-start(bf16[512,768]{1,0:T(8,128)(2,1)} %bitcast.6), channel_id=1, source_target_pairs={{0,8},{4,12},{1,9},{5,13},{2,10},{6,14},{3,11},{7,15},{16,24},{20,... | collective-permute-start | bytes 2359304 | tf_op jit(solution)/shard_map/ppermute | solution.py:212
  19.0 0.0 copy-start.1
  19.0 2.0 %copy.14 = bf16[1,4,333,768]{3,2,1,0:T(8,128)(2,1)S(1)} copy(bf16[1,4,333,768]{3,1,2,0:T(4,128)(2,1)} %param.11) | data formatting | bytes 4091904 | tf_op args[3]
  21.0 0.2 copy-done.1
  21.2 0.3 copy.13
  21.4 1.6 pad.7.k_ref
  23.0 0.0 copy-start.9
  23.0 0.0 copy-start.2
  23.0 1.6 pad.8.v_ref
  24.6 0.0 copy-done.9
  24.6 0.2 reduce-window.9
  24.8 0.0 copy-start.4
  24.8 0.0 copy-done.2
  24.8 0.6 add_add_fusion.4
  25.4 0.7 add_add_fusion.5
  26.1 23.8 %shard_map.82 = (f32[12,512,1]{2,1,0:T(8,128)}, f32[12,512,1]{2,1,0:T(8,128)}, f32[512,768]{1,0:T(8,128)}) custom-call(s32[10]{0:T(128)} %get-tuple-element.35.info_ref, bf16[512,768]{1,0:T(8,128)(2,1)} %bitcast.44, bf16[4,384,768]{2,1,0:T(8,128)(2,1)} %pad.7.k_ref, bf16[4,384,768]{2,1,0:T(8,128)(2,1)} %pad.8.v_ref), custom_call_target="tpu_custom_call" | custom-call | flops 154618822656 | bytes 14155776 | tf_op jit(solution)/shard_map/pallas_call | solution.py:158
  49.9 0.0 copy-done.4
  49.9 0.0 copy-start.3
  49.9 0.0 copy-start.5
  49.9 0.0 copy-start.6
  49.9 23.5 %shard_map.83 = (f32[12,512,1]{2,1,0:T(8,128)}, f32[12,512,1]{2,1,0:T(8,128)}, f32[512,768]{1,0:T(8,128)}) custom-call(s32[10]{0:T(128)} %get-tuple-element.37.info_ref, bf16[512,768]{1,0:T(8,128)(2,1)} %bitcast.45, bf16[2,256,768]{2,1,0:T(8,128)(2,1)} %bitcast.19.k_ref, bf16[2,256,768]{2,1,0:T(8,128)(2,1)} %bitcast.41, ...), custom_call_target="tpu_custom_call" | custom-call | flops 51539607552 | bytes 7864320 | tf_op jit(solution)/shard_map/pallas_call | solution.py:158
  73.5 0.0 copy-done.3
  73.5 0.0 copy-done.5
  73.5 0.7 add_add_fusion.3
  74.1 0.0 collective-permute-done.6
  74.1 0.0 copy-done.6
  74.1 1.3 collective-permute-start.3
  75.5 0.0 collective-permute-done.7
  75.5 1.5 collective-permute-start
  77.0 9.9 %shard_map.84 = (f32[12,512,1]{2,1,0:T(8,128)}, f32[12,512,1]{2,1,0:T(8,128)}, f32[512,768]{1,0:T(8,128)}) custom-call(s32[10]{0:T(128)} %get-tuple-element.39.info_ref, bf16[512,768]{1,0:T(8,128)(2,1)} %bitcast.46, bf16[2,256,768]{2,1,0:T(8,128)(2,1)} %bitcast.17.k_ref, bf16[2,256,768]{2,1,0:T(8,128)(2,1)} %bitcast.18.v_ref, ...), custom_call_target="tpu_custom_call" | custom-call | flops 51539607552 | bytes 7864320 | tf_op jit(solution)/shard_map/pallas_call | solution.py:158
  86.8 0.0 collective-permute-done.4
  86.8 1.3 collective-permute-start.1
  88.1 0.0 collective-permute-done.5
  88.2 18.3 %shard_map.85 = (f32[12,512,1]{2,1,0:T(8,128)}, f32[12,512,1]{2,1,0:T(8,128)}, f32[512,768]{1,0:T(8,128)}) custom-call(s32[10]{0:T(128)} %get-tuple-element.38.info_ref, bf16[512,768]{1,0:T(8,128)(2,1)} %bitcast.47, bf16[2,256,768]{2,1,0:T(8,128)(2,1)} %bitcast.14.k_ref, bf16[2,256,768]{2,1,0:T(8,128)(2,1)} %bitcast.15.v_ref, ...), custom_call_target="tpu_custom_call" | custom-call | flops 51539607552 | bytes 7864320 | tf_op jit(solution)/shard_map/pallas_call | solution.py:158
  106.5 0.0 collective-permute-done.2
  106.5 0.0 collective-permute-done.3
  106.5 0.0 copy-start.7
  106.5 0.9 copy-done.7
  107.4 9.9 %shard_map.86 = (f32[12,512,1]{2,1,0:T(8,128)}, f32[12,512,1]{2,1,0:T(8,128)}, f32[512,768]{1,0:T(8,128)}) custom-call(s32[10]{0:T(128)} %get-tuple-element.36.info_ref, bf16[512,768]{1,0:T(8,128)(2,1)} %bitcast.48, bf16[2,256,768]{2,1,0:T(8,128)(2,1)} %bitcast.11.k_ref, bf16[2,256,768]{2,1,0:T(8,128)(2,1)} %bitcast.50, ...), custom_call_target="tpu_custom_call" | custom-call | flops 51539607552 | bytes 7864320 | tf_op jit(solution)/shard_map/pallas_call | solution.py:158
  117.3 15.1 %collective-permute-done = bf16[512,768]{1,0:T(8,128)(2,1)} collective-permute-done((bf16[512,768]{1,0:T(8,128)(2,1)}, bf16[512,768]{1,0:T(8,128)(2,1)}, u32[]{:S(2)}, u32[]{:S(2)}) %collective-permute-start) | collective-permute-done | bytes 786464 | tf_op jit(solution)/shard_map/ppermute | solution.py:212
  132.3 14.9 %collective-permute-done.1 = bf16[512,768]{1,0:T(8,128)(2,1)S(1)} collective-permute-done((bf16[512,768]{1,0:T(8,128)(2,1)S(1)}, bf16[512,768]{1,0:T(8,128)(2,1)S(1)}, u32[]{:S(2)}, u32[]{:S(2)}) %collective-permute-start.1) | collective-permute-done | bytes 786464 | tf_op jit(solution)/shard_map/ppermute | solution.py:213
  147.2 0.0 copy-start.8
  147.2 0.9 copy-done.8
  148.2 7.9 %shard_map.87 = bf16[512,768]{1,0:T(8,128)(2,1)} custom-call(s32[10]{0:T(128)} %get-tuple-element.40.info_ref, bf16[512,768]{1,0:T(8,128)(2,1)} %bitcast.49, bf16[2,256,768]{2,1,0:T(8,128)(2,1)} %bitcast.7.k_ref, bf16[2,256,768]{2,1,0:T(8,128)(2,1)} %bitcast.51, f32[12,512,1]{2,1,0:T(8,128)} %get-tuple-element.32.refs_0_, ...), custom_call_target="tpu_custom_call" | custom-call | flops 51539607552 | bytes 7864320 | tf_op jit(solution)/shard_map/pallas_call | solution.py:158
  156.0 1.5 collective-permute-start.8
  157.5 2.2 %fusion.2 = f32[512,608]{0,1:T(8,128)S(1)} fusion(bf16[512,768]{1,0:T(8,128)(2,1)} %shard_map.87, bf16[1536,1216]{0,1:T(8,128)(2,1)} %param.15, s32[]{:T(128)S(6)} %select_n.28, s32[]{:T(128)S(6)} %select_n.34), kind=kOutput, calls=%fused_computation.6 | convolution fusion | flops 478150656 | bytes 2965512 | tf_op jit(solution)/shard_map/dot_general | solution.py:243
  159.7 14.2 %collective-permute-done.8 = bf16[512,768]{1,0:T(8,128)(2,1)S(1)} collective-permute-done((bf16[512,768]{1,0:T(8,128)(2,1)}, bf16[512,768]{1,0:T(8,128)(2,1)S(1)}, u32[]{:S(2)}, u32[]{:S(2)}) %collective-permute-start.8) | collective-permute-done | bytes 786464 | tf_op jit(solution)/shard_map/ppermute | solution.py:19
  173.9 1.9 %fusion = f32[512,608]{0,1:T(8,128)S(1)} fusion(bf16[512,768]{1,0:T(8,128)(2,1)S(1)} %collective-permute-done.8, bf16[1536,1216]{0,1:T(8,128)(2,1)} %param.15, s32[]{:T(128)S(6)} %select_n.32, s32[]{:T(128)S(6)} %select_n.34), kind=kOutput, calls=%fused_computation.4 | convolution fusion | flops 478150656 | bytes 2965512 | tf_op jit(solution)/shard_map/dot_general | solution.py:244
  175.8 0.0 copy-start
  175.8 0.3 add_convert_fusion.1
  176.1 0.1 collective-permute-start.9
  176.2 0.7 copy-done
  176.9 1.9 %fusion.6 = f32[512,608]{0,1:T(8,128)S(1)} fusion(bf16[512,768]{1,0:T(8,128)(2,1)S(1)} %copy-done, bf16[1536,1216]{0,1:T(8,128)(2,1)} %param.15, s32[]{:T(128)S(6)} %select_n.28, s32[]{:T(128)S(6)} %select_n.30), kind=kOutput, calls=%fused_computation.10 | convolution fusion | flops 478150656 | bytes 2965512 | tf_op jit(solution)/shard_map/dot_general | solution.py:243
  178.9 1.9 %fusion.4 = f32[512,608]{0,1:T(8,128)S(1)} fusion(bf16[512,768]{1,0:T(8,128)(2,1)S(1)} %collective-permute-done.8, bf16[1536,1216]{0,1:T(8,128)(2,1)} %param.15, s32[]{:T(128)S(6)} %select_n.32, s32[]{:T(128)S(6)} %select_n.30), kind=kOutput, calls=%fused_computation.8 | convolution fusion | flops 478150656 | bytes 2965512 | tf_op jit(solution)/shard_map/dot_general | solution.py:244
  180.8 0.0 collective-permute-done.9
  180.8 1.2 add_convert_fusion
Async XLA Ops:
  0.0 74.1 %collective-permute-start.6 = (bf16[512,768]{1,0:T(8,128)(2,1)}, bf16[512,768]{1,0:T(8,128)(2,1)}, u32[]{:S(2)}, u32[]{:S(2)}) collective-permute-start(bf16[512,768]{1,0:T(8,128)(2,1)} %bitcast.6), channel_id=1, source_target_pairs={{0,4},{4,8},{8,12},{1,5},{5,9},{9,13},{2,6},{6,10},{10,14},{3,7},{... | collective-permute-start | bytes 2359304 | tf_op jit(solution)/shard_map/ppermute | solution.py:212
  5.8 81.1 %collective-permute-start.4 = (bf16[512,768]{1,0:T(8,128)(2,1)}, bf16[512,768]{1,0:T(8,128)(2,1)}, u32[]{:S(2)}, u32[]{:S(2)}) collective-permute-start(bf16[512,768]{1,0:T(8,128)(2,1)} %bitcast.6), channel_id=1, source_target_pairs={{4,0},{8,4},{12,8},{5,1},{9,5},{13,9},{6,2},{10,6},{14,10},{7,3},{... | collective-permute-start | bytes 2359304 | tf_op jit(solution)/shard_map/ppermute | solution.py:212
  7.1 68.4 %collective-permute-start.7 = (bf16[512,768]{1,0:T(8,128)(2,1)}, bf16[512,768]{1,0:T(8,128)(2,1)}, u32[]{:S(2)}, u32[]{:S(2)}) collective-permute-start(bf16[512,768]{1,0:T(8,128)(2,1)} %bitcast.39), channel_id=1, source_target_pairs={{0,4},{4,8},{8,12},{1,5},{5,9},{9,13},{2,6},{6,10},{10,14},{3,7},{... | collective-permute-start | bytes 2359304 | tf_op jit(solution)/shard_map/ppermute | solution.py:213
  12.5 75.6 %collective-permute-start.5 = (bf16[512,768]{1,0:T(8,128)(2,1)}, bf16[512,768]{1,0:T(8,128)(2,1)}, u32[]{:S(2)}, u32[]{:S(2)}) collective-permute-start(bf16[512,768]{1,0:T(8,128)(2,1)} %bitcast.40), channel_id=1, source_target_pairs={{4,0},{8,4},{12,8},{5,1},{9,5},{13,9},{6,2},{10,6},{14,10},{7,3},{... | collective-permute-start | bytes 2359304 | tf_op jit(solution)/shard_map/ppermute | solution.py:213
  13.8 92.7 %collective-permute-start.2 = (bf16[512,768]{1,0:T(8,128)(2,1)}, bf16[512,768]{1,0:T(8,128)(2,1)}, u32[]{:S(2)}, u32[]{:S(2)}) collective-permute-start(bf16[512,768]{1,0:T(8,128)(2,1)} %bitcast.6), channel_id=1, source_target_pairs={{0,8},{4,12},{1,9},{5,13},{2,10},{6,14},{3,11},{7,15},{16,24},{20,... | collective-permute-start | bytes 2359304 | tf_op jit(solution)/shard_map/ppermute | solution.py:212
  19.0 2.2 %copy-start.1 = (bf16[1,4,333,768]{3,1,2,0:T(4,128)(2,1)S(1)}, bf16[1,4,333,768]{3,1,2,0:T(4,128)(2,1)}, u32[]{:S(2)}) copy-start(bf16[1,4,333,768]{3,1,2,0:T(4,128)(2,1)} %param.12) | copy-start | bytes 6137860
  23.0 1.6 copy-start.9
  23.0 1.8 copy-start.2
  24.8 25.1 %copy-start.4 = (s32[4,1]{0,1:T(1,128)}, s32[4,1]{0,1:T(1,128)S(1)}, u32[]{:S(2)}) copy-start(s32[4,1]{0,1:T(1,128)S(1)} %reduce-window.9) | copy-start | bytes 52
  49.9 23.6 %copy-start.3 = (s32[1,4]{1,0:T(1,128)S(1)}, s32[1,4]{1,0:T(1,128)}, u32[]{:S(2)}) copy-start(s32[1,4]{1,0:T(1,128)} %param.13) | copy-start | bytes 52
  49.9 23.6 %copy-start.5 = (s32[4,1]{0,1:T(1,128)S(1)}, s32[4,1]{0,1:T(1,128)}, u32[]{:S(2)}) copy-start(s32[4,1]{0,1:T(1,128)} %copy-done.4) | copy-start | bytes 52
  49.9 24.2 %copy-start.6 = (bf16[1,512,768]{2,1,0:T(8,128)(2,1)S(1)}, bf16[1,512,768]{2,1,0:T(8,128)(2,1)}, u32[]{:S(2)}) copy-start(bf16[1,512,768]{2,1,0:T(8,128)(2,1)} %param.10) | copy-start | bytes 2359300
  74.1 32.4 %collective-permute-start.3 = (bf16[512,768]{1,0:T(8,128)(2,1)S(1)}, bf16[512,768]{1,0:T(8,128)(2,1)S(1)}, u32[]{:S(2)}, u32[]{:S(2)}) collective-permute-start(bf16[512,768]{1,0:T(8,128)(2,1)S(1)} %bitcast.42), channel_id=1, source_target_pairs={{0,8},{4,12},{1,9},{5,13},{2,10},{6,14},{3,11},{7,15},{16,24},{20,... | collective-permute-start | bytes 2359304 | tf_op jit(solution)/shard_map/ppermute | solution.py:213
  75.5 56.9 %collective-permute-start = (bf16[512,768]{1,0:T(8,128)(2,1)}, bf16[512,768]{1,0:T(8,128)(2,1)}, u32[]{:S(2)}, u32[]{:S(2)}) collective-permute-start(bf16[512,768]{1,0:T(8,128)(2,1)} %bitcast.6), channel_id=1, source_target_pairs={{8,0},{12,4},{9,1},{13,5},{10,2},{14,6},{11,3},{15,7},{24,16},{28,... | collective-permute-start | bytes 2359304 | tf_op jit(solution)/shard_map/ppermute | solution.py:212
  86.8 60.4 %collective-permute-start.1 = (bf16[512,768]{1,0:T(8,128)(2,1)S(1)}, bf16[512,768]{1,0:T(8,128)(2,1)S(1)}, u32[]{:S(2)}, u32[]{:S(2)}) collective-permute-start(bf16[512,768]{1,0:T(8,128)(2,1)S(1)} %bitcast.43), channel_id=1, source_target_pairs={{8,0},{12,4},{9,1},{13,5},{10,2},{14,6},{11,3},{15,7},{24,16},{28,... | collective-permute-start | bytes 2359304 | tf_op jit(solution)/shard_map/ppermute | solution.py:213
  106.5 0.9 copy-start.7
  147.2 0.9 copy-start.8
  156.0 17.9 %collective-permute-start.8 = (bf16[512,768]{1,0:T(8,128)(2,1)}, bf16[512,768]{1,0:T(8,128)(2,1)S(1)}, u32[]{:S(2)}, u32[]{:S(2)}) collective-permute-start(bf16[512,768]{1,0:T(8,128)(2,1)} %shard_map.87), channel_id=1, source_target_pairs={{0,2},{2,0},{1,3},{3,1},{4,6},{6,4},{5,7},{7,5},{8,10},{10,8},{9,1... | collective-permute-start | bytes 2359304 | tf_op jit(solution)/shard_map/ppermute | solution.py:19
  175.8 1.1 copy-start
  176.1 4.7 %collective-permute-start.9 = (bf16[512,608]{0,1:T(8,128)(2,1)S(1)}, bf16[512,608]{0,1:T(8,128)(2,1)S(1)}, u32[]{:S(2)}, u32[]{:S(2)}) collective-permute-start(bf16[512,608]{0,1:T(8,128)(2,1)S(1)} %add_convert_fusion.1), channel_id=1, source_target_pairs={{0,1},{1,0},{2,3},{3,2},{4,5},{5,4},{6,7},{7,6},{8,9},{9,8},{10,11... | collective-permute-start | bytes 1867784 | tf_op jit(solution)/shard_map/ppermute | solution.py:19

commit v2 on v1

--- a/solution.py
+++ b/solution.py
@@ -203,17 +203,13 @@
     common = dict(reqs=reqs, total=total)
     state = attend_chunk(info_for(0), queries, text_k, text_v, None, kind="text", last=False, **common)
     chunks = [(k_img[0], v_img[0], me * tok_dev)]
+    both = jnp.stack([k_img[0], v_img[0]])
     for step in range(1, reach + 1):
         to_right = [(i, i + step) for i in range(nseq - step)]
         to_left = [(i + step, i) for i in range(nseq - step)]
         for pairs, sign in ((to_right, -1), (to_left, 1)):
-            chunks.append(
-                (
-                    lax.ppermute(k_img[0], "seq", pairs),
-                    lax.ppermute(v_img[0], "seq", pairs),
-                    (me + sign * step) * tok_dev,
-                )
-            )
+            got = lax.ppermute(both, "seq", pairs)
+            chunks.append((got[0], got[1], (me + sign * step) * tok_dev))
     for index, (key_rows, val_rows, lower) in enumerate(chunks):
         state = attend_chunk(
             info_for(lower),

time: 181 us -> 169 us (0.934)
  the two profiles are of different devices: /device:TPU:0 before, /device:TPU:15 now
where the time goes in v2:
time: 169 us
  Pallas kernels  108 us (64%)
  starting transfers between devices  19.9 us (12%)
  local copies, waits for them, and re-layouts  18.8 us (11%)
  waiting for transfers between devices  11.2 us (7%)
  matrix products  7.89 us (5%)
  other arithmetic  3.35 us (2%)
    pallas_call x6, Pallas kernels, attend_chunk(): pl.pallas_call(kernel, out_shape=out_shape, grid_spec=pltpu.PrefetchScala...  108 us
    ppermute x4, starting transfers between devices, local(): got = lax.ppermute(both, 'seq', pairs)  13.1 us
    ppermute x2, waiting for transfers between devices, partner_2(): lax.ppermute(x, axis, [(i, i ^ 1 << distance) for i in range(lax.axis_siz...  11.2 us
    slice x4, local copies, waits for them, and re-layouts, local(): chunks.append((got[0], got[1], (me + sign * step) * tok_dev))  10.6 us
    ppermute x2, starting transfers between devices, partner_2(): lax.ppermute(x, axis, [(i, i ^ 1 << distance) for i in range(lax.axis_siz...  6.88 us
    unnamed x21, local copies, waits for them, and re-layouts  4.08 us
    dot_general x2, matrix products, project(): jnp.dot(attn, w_mine, preferred_element_type=jnp.float32)  4 us
    dot_general x2, matrix products, project(): return own + jnp.dot(other, w_other, preferred_element_type=jnp.float32)  3.89 us
  transfers between devices with their start and end apart: 6, of which 1 were waited for; matrix products, arithmetic and copies ran while one was open for 12% of the time, Pallas kernels for 54%

profile of v2, /device:TPU:15, one launch (start us, length us, event | category | flops | bytes accessed | tf_op | source)
XLA Modules:
  0.0 169.5 jit_solution(9832264112476278587)
XLA Ops:
  0.0 0.0 copy-start.3
  0.0 0.0 copy-start.1
  0.0 2.2 %constant_dynamic-update-slice_fusion.1 = bf16[2,512,768]{2,1,0:T(8,128)(2,1)} fusion(bf16[1,512,768]{2,1,0:T(8,128)(2,1)} %param.9), kind=kLoop, calls=%fused_computation.13 | loop fusion | bytes 1572864
  2.2 0.0 copy-done.3
  2.2 0.9 constant_dynamic-update-slice_fusion
  3.2 3.2 %collective-permute-start.3 = (bf16[2,512,768]{2,1,0:T(8,128)(2,1)}, bf16[2,512,768]{2,1,0:T(8,128)(2,1)}, u32[]{:S(2)}, u32[]{:S(2)}) collective-permute-start(bf16[2,512,768]{2,1,0:T(8,128)(2,1)} %constant_dynamic-update-slice_fusion), channel_id=1, source_target_pairs={{0,4},{4,8},{8,12},{1,5},{5,9},{9,13},{2,6},{6,10},{10,14},{3,7},{... | collective-permute-start | bytes 4718600 | tf_op jit(solution)/shard_map/ppermute | solution.py:211
  6.4 3.2 %collective-permute-start.2 = (bf16[2,512,768]{2,1,0:T(8,128)(2,1)}, bf16[2,512,768]{2,1,0:T(8,128)(2,1)}, u32[]{:S(2)}, u32[]{:S(2)}) collective-permute-start(bf16[2,512,768]{2,1,0:T(8,128)(2,1)} %constant_dynamic-update-slice_fusion), channel_id=1, source_target_pairs={{4,0},{8,4},{12,8},{5,1},{9,5},{13,9},{6,2},{10,6},{14,10},{7,3},{... | collective-permute-start | bytes 4718600 | tf_op jit(solution)/shard_map/ppermute | solution.py:211
  9.6 5.4 %collective-permute-start.1 = (bf16[2,512,768]{2,1,0:T(8,128)(2,1)}, bf16[2,512,768]{2,1,0:T(8,128)(2,1)}, u32[]{:S(2)}, u32[]{:S(2)}) collective-permute-start(bf16[2,512,768]{2,1,0:T(8,128)(2,1)} %constant_dynamic-update-slice_fusion), channel_id=1, source_target_pairs={{0,8},{4,12},{1,9},{5,13},{2,10},{6,14},{3,11},{7,15},{16,24},{20,... | collective-permute-start | bytes 4718600 | tf_op jit(solution)/shard_map/ppermute | solution.py:211
  15.0 1.3 collective-permute-start
  16.3 0.0 copy-done.1
  16.3 0.0 copy-start.2
  16.3 0.3 copy.14
  16.6 1.3 copy-done.2
  17.9 0.3 copy.13
  18.1 1.6 pad.7.k_ref
  19.7 0.0 copy-start.8
  19.7 0.0 copy-start.4
  19.7 1.6 pad.8.v_ref
  21.3 0.0 copy-done.8
  21.3 0.2 reduce-window.9
  21.5 0.0 copy-start.6
  21.5 0.0 copy-done.4
  21.5 0.6 add_add_fusion.4
  22.1 0.7 add_add_fusion.5
  22.8 23.5 %shard_map.82 = (f32[12,512,1]{2,1,0:T(8,128)}, f32[12,512,1]{2,1,0:T(8,128)}, f32[512,768]{1,0:T(8,128)}) custom-call(s32[10]{0:T(128)} %get-tuple-element.43.info_ref, bf16[512,768]{1,0:T(8,128)(2,1)} %bitcast.47, bf16[4,384,768]{2,1,0:T(8,128)(2,1)} %pad.7.k_ref, bf16[4,384,768]{2,1,0:T(8,128)(2,1)} %pad.8.v_ref), custom_call_target="tpu_custom_call" | custom-call | flops 154618822656 | bytes 14155776 | tf_op jit(solution)/shard_map/pallas_call | solution.py:158
  46.3 0.0 copy-done.6
  46.3 0.0 copy-start.5
  46.3 0.0 copy-start.7
  46.3 23.5 %shard_map.83 = (f32[12,512,1]{2,1,0:T(8,128)}, f32[12,512,1]{2,1,0:T(8,128)}, f32[512,768]{1,0:T(8,128)}) custom-call(s32[10]{0:T(128)} %get-tuple-element.45.info_ref, bf16[512,768]{1,0:T(8,128)(2,1)} %bitcast.48, bf16[2,256,768]{2,1,0:T(8,128)(2,1)} %bitcast.31, bf16[2,256,768]{2,1,0:T(8,128)(2,1)} %bitcast.32, f32[12,512,1]{2,1,0:T(8,128)} %get-tuple-element.20.refs_0_, ...), custom_call_target="tpu_custom_call" | custom-call | flops 51539607552 | bytes 7864320 | tf_op jit(solution)/shard_map/pallas_call | solution.py:158
  69.8 0.0 copy-done.5
  69.8 0.0 copy-done.7
  69.8 0.6 add_add_fusion.3
  70.5 0.0 collective-permute-done.3
  70.5 2.7 %fusion.8 = (bf16[1,512,768]{2,1,0:T(8,128)(2,1)}, bf16[1,512,768]{2,1,0:T(8,128)(2,1)}) fusion(bf16[2,512,768]{2,1,0:T(8,128)(2,1)} %collective-permute-done.3), kind=kLoop, calls=%fused_computation.20 | loop fusion | bytes 3145728 | tf_op jit(solution)/shard_map/slice | solution.py:212
  73.2 16.5 %shard_map.84 = (f32[12,512,1]{2,1,0:T(8,128)}, f32[12,512,1]{2,1,0:T(8,128)}, f32[512,768]{1,0:T(8,128)}) custom-call(s32[10]{0:T(128)} %get-tuple-element.47.info_ref, bf16[512,768]{1,0:T(8,128)(2,1)} %bitcast.49, bf16[2,256,768]{2,1,0:T(8,128)(2,1)} %bitcast.38, bf16[2,256,768]{2,1,0:T(8,128)(2,1)} %bitcast.37, f32[12,512,1]{2,1,0:T(8,128)} %get-tuple-element.23.refs_0_, ...), custom_call_target="tpu_custom_call" | custom-call | flops 51539607552 | bytes 7864320 | tf_op jit(solution)/shard_map/pallas_call | solution.py:158
  89.7 0.0 collective-permute-done.2
  89.7 2.6 %fusion.9 = (bf16[1,512,768]{2,1,0:T(8,128)(2,1)}, bf16[1,512,768]{2,1,0:T(8,128)(2,1)}) fusion(bf16[2,512,768]{2,1,0:T(8,128)(2,1)} %collective-permute-done.2), kind=kLoop, calls=%fused_computation.21 | loop fusion | bytes 3145728 | tf_op jit(solution)/shard_map/slice | solution.py:212
  92.3 18.3 %shard_map.85 = (f32[12,512,1]{2,1,0:T(8,128)}, f32[12,512,1]{2,1,0:T(8,128)}, f32[512,768]{1,0:T(8,128)}) custom-call(s32[10]{0:T(128)} %get-tuple-element.46.info_ref, bf16[512,768]{1,0:T(8,128)(2,1)} %bitcast.50, bf16[2,256,768]{2,1,0:T(8,128)(2,1)} %bitcast.34, bf16[2,256,768]{2,1,0:T(8,128)(2,1)} %bitcast.33, f32[12,512,1]{2,1,0:T(8,128)} %get-tuple-element.26.refs_0_, ...), custom_call_target="tpu_custom_call" | custom-call | flops 51539607552 | bytes 7864320 | tf_op jit(solution)/shard_map/pallas_call | solution.py:158
  110.7 0.0 collective-permute-done.1
  110.7 2.7 %fusion.10 = (bf16[1,512,768]{2,1,0:T(8,128)(2,1)}, bf16[1,512,768]{2,1,0:T(8,128)(2,1)}) fusion(bf16[2,512,768]{2,1,0:T(8,128)(2,1)} %collective-permute-done.1), kind=kLoop, calls=%fused_computation.22 | loop fusion | bytes 3145728 | tf_op jit(solution)/shard_map/slice | solution.py:212
  113.3 10.1 %shard_map.86 = (f32[12,512,1]{2,1,0:T(8,128)}, f32[12,512,1]{2,1,0:T(8,128)}, f32[512,768]{1,0:T(8,128)}) custom-call(s32[10]{0:T(128)} %get-tuple-element.44.info_ref, bf16[512,768]{1,0:T(8,128)(2,1)} %bitcast.51, bf16[2,256,768]{2,1,0:T(8,128)(2,1)} %bitcast.36, bf16[2,256,768]{2,1,0:T(8,128)(2,1)} %bitcast.35, f32[12,512,1]{2,1,0:T(8,128)} %get-tuple-element.29.refs_0_, ...), custom_call_target="tpu_custom_call" | custom-call | flops 51539607552 | bytes 7864320 | tf_op jit(solution)/shard_map/pallas_call | solution.py:158
  123.4 0.0 collective-permute-done
  123.4 2.6 %fusion.11 = (bf16[1,512,768]{2,1,0:T(8,128)(2,1)}, bf16[1,512,768]{2,1,0:T(8,128)(2,1)}) fusion(bf16[2,512,768]{2,1,0:T(8,128)(2,1)} %collective-permute-done), kind=kLoop, calls=%fused_computation.23 | loop fusion | bytes 3145728 | tf_op jit(solution)/shard_map/slice | solution.py:212
  126.1 16.1 %shard_map.87 = bf16[512,768]{1,0:T(8,128)(2,1)} custom-call(s32[10]{0:T(128)} %get-tuple-element.48.info_ref, bf16[512,768]{1,0:T(8,128)(2,1)} %bitcast.52, bf16[2,256,768]{2,1,0:T(8,128)(2,1)} %bitcast.40, bf16[2,256,768]{2,1,0:T(8,128)(2,1)} %bitcast.39, f32[12,512,1]{2,1,0:T(8,128)} %get-tuple-element.32.refs_0_, ...), custom_call_target="tpu_custom_call" | custom-call | flops 51539607552 | bytes 7864320 | tf_op jit(solution)/shard_map/pallas_call | solution.py:158
  142.2 0.2 collective-permute-start.4
  142.5 2.1 %fusion.2 = f32[512,608]{0,1:T(8,128)S(1)} fusion(bf16[512,768]{1,0:T(8,128)(2,1)} %shard_map.87, bf16[1536,1216]{0,1:T(8,128)(2,1)} %param.15, s32[]{:T(128)S(6)} %select_n.28, s32[]{:T(128)S(6)} %select_n.34), kind=kOutput, calls=%fused_computation.6 | convolution fusion | flops 478150656 | bytes 2965512 | tf_op jit(solution)/shard_map/dot_general | solution.py:239
  144.6 0.0 copy-start
  144.6 11.2 %collective-permute-done.4 = bf16[512,768]{1,0:T(8,128)(2,1)S(1)} collective-permute-done((bf16[512,768]{1,0:T(8,128)(2,1)}, bf16[512,768]{1,0:T(8,128)(2,1)S(1)}, u32[]{:S(2)}, u32[]{:S(2)}) %collective-permute-start.4) | collective-permute-done | bytes 786464 | tf_op jit(solution)/shard_map/ppermute | solution.py:19
  155.8 1.9 %add_convert_fusion.1 = bf16[512,608]{0,1:T(8,128)(2,1)S(1)} fusion(f32[512,608]{0,1:T(8,128)S(1)} %fusion.2, bf16[512,768]{1,0:T(8,128)(2,1)S(1)} %collective-permute-done.4, bf16[1536,1216]{0,1:T(8,128)(2,1)} %param.15, s32[]{:T(128)S(6)} %select_n.32, s32[]{:T(128)S(6)} %select_n.34), kind=kOutput, calls=%fused_computation.3 | convolution fusion | flops 478773248 | bytes 3588104 | tf_op jit(solution)/shard_map/dot_general | solution.py:240
  157.8 6.6 %collective-permute-start.5 = (bf16[512,608]{0,1:T(8,128)(2,1)S(1)}, bf16[512,608]{0,1:T(8,128)(2,1)S(1)}, u32[]{:S(2)}, u32[]{:S(2)}) collective-permute-start(bf16[512,608]{0,1:T(8,128)(2,1)S(1)} %add_convert_fusion.1), channel_id=1, source_target_pairs={{0,1},{1,0},{2,3},{3,2},{4,5},{5,4},{6,7},{7,6},{8,9},{9,8},{10,11... | collective-permute-start | bytes 1867784 | tf_op jit(solution)/shard_map/ppermute | solution.py:19
  164.4 0.0 copy-done
  164.4 1.9 %fusion.6 = f32[512,608]{0,1:T(8,128)S(1)} fusion(bf16[512,768]{1,0:T(8,128)(2,1)S(1)} %copy-done, bf16[1536,1216]{0,1:T(8,128)(2,1)} %param.15, s32[]{:T(128)S(6)} %select_n.28, s32[]{:T(128)S(6)} %select_n.30), kind=kOutput, calls=%fused_computation.10 | convolution fusion | flops 478150656 | bytes 2965512 | tf_op jit(solution)/shard_map/dot_general | solution.py:239
  166.3 1.9 %fusion.4 = f32[512,608]{0,1:T(8,128)S(1)} fusion(bf16[512,768]{1,0:T(8,128)(2,1)S(1)} %collective-permute-done.4, bf16[1536,1216]{0,1:T(8,128)(2,1)} %param.15, s32[]{:T(128)S(6)} %select_n.32, s32[]{:T(128)S(6)} %select_n.30), kind=kOutput, calls=%fused_computation.8 | convolution fusion | flops 478150656 | bytes 2965512 | tf_op jit(solution)/shard_map/dot_general | solution.py:240
  168.2 0.0 collective-permute-done.5
  168.2 1.2 add_convert_fusion
Async XLA Ops:
  0.0 2.2 %copy-start.3 = (bf16[1,512,768]{2,1,0:T(8,128)(2,1)S(1)}, bf16[1,512,768]{2,1,0:T(8,128)(2,1)}, u32[]{:S(2)}) copy-start(bf16[1,512,768]{2,1,0:T(8,128)(2,1)} %param.10) | copy-start | bytes 2359300
  0.0 16.3 %copy-start.1 = (bf16[1,4,333,768]{3,1,2,0:T(4,128)(2,1)S(1)}, bf16[1,4,333,768]{3,1,2,0:T(4,128)(2,1)}, u32[]{:S(2)}) copy-start(bf16[1,4,333,768]{3,1,2,0:T(4,128)(2,1)} %param.11) | copy-start | bytes 6137860
  3.2 67.3 %collective-permute-start.3 = (bf16[2,512,768]{2,1,0:T(8,128)(2,1)}, bf16[2,512,768]{2,1,0:T(8,128)(2,1)}, u32[]{:S(2)}, u32[]{:S(2)}) collective-permute-start(bf16[2,512,768]{2,1,0:T(8,128)(2,1)} %constant_dynamic-update-slice_fusion), channel_id=1, source_target_pairs={{0,4},{4,8},{8,12},{1,5},{5,9},{9,13},{2,6},{6,10},{10,14},{3,7},{... | collective-permute-start | bytes 4718600 | tf_op jit(solution)/shard_map/ppermute | solution.py:211
  6.4 83.3 %collective-permute-start.2 = (bf16[2,512,768]{2,1,0:T(8,128)(2,1)}, bf16[2,512,768]{2,1,0:T(8,128)(2,1)}, u32[]{:S(2)}, u32[]{:S(2)}) collective-permute-start(bf16[2,512,768]{2,1,0:T(8,128)(2,1)} %constant_dynamic-update-slice_fusion), channel_id=1, source_target_pairs={{4,0},{8,4},{12,8},{5,1},{9,5},{13,9},{6,2},{10,6},{14,10},{7,3},{... | collective-permute-start | bytes 4718600 | tf_op jit(solution)/shard_map/ppermute | solution.py:211
  9.6 101.0 %collective-permute-start.1 = (bf16[2,512,768]{2,1,0:T(8,128)(2,1)}, bf16[2,512,768]{2,1,0:T(8,128)(2,1)}, u32[]{:S(2)}, u32[]{:S(2)}) collective-permute-start(bf16[2,512,768]{2,1,0:T(8,128)(2,1)} %constant_dynamic-update-slice_fusion), channel_id=1, source_target_pairs={{0,8},{4,12},{1,9},{5,13},{2,10},{6,14},{3,11},{7,15},{16,24},{20,... | collective-permute-start | bytes 4718600 | tf_op jit(solution)/shard_map/ppermute | solution.py:211
  15.0 108.4 %collective-permute-start = (bf16[2,512,768]{2,1,0:T(8,128)(2,1)}, bf16[2,512,768]{2,1,0:T(8,128)(2,1)}, u32[]{:S(2)}, u32[]{:S(2)}) collective-permute-start(bf16[2,512,768]{2,1,0:T(8,128)(2,1)} %constant_dynamic-update-slice_fusion), channel_id=1, source_target_pairs={{8,0},{12,4},{9,1},{13,5},{10,2},{14,6},{11,3},{15,7},{24,16},{28,... | collective-permute-start | bytes 4718600 | tf_op jit(solution)/shard_map/ppermute | solution.py:211
  16.3 1.6 copy-start.2
  19.7 1.6 copy-start.8
  19.7 1.8 %copy-start.4 = (s32[1,4]{1,0:T(1,128)S(1)}, s32[1,4]{1,0:T(1,128)}, u32[]{:S(2)}) copy-start(s32[1,4]{1,0:T(1,128)} %param.13) | copy-start | bytes 52
  21.5 24.8 %copy-start.6 = (s32[4,1]{0,1:T(1,128)}, s32[4,1]{0,1:T(1,128)S(1)}, u32[]{:S(2)}) copy-start(s32[4,1]{0,1:T(1,128)S(1)} %reduce-window.9) | copy-start | bytes 52
  46.3 23.5 %copy-start.5 = (s32[1,4]{1,0:T(1,128)S(1)}, s32[1,4]{1,0:T(1,128)}, u32[]{:S(2)}) copy-start(s32[1,4]{1,0:T(1,128)} %param.13) | copy-start | bytes 52
  46.3 23.5 %copy-start.7 = (s32[4,1]{0,1:T(1,128)S(1)}, s32[4,1]{0,1:T(1,128)}, u32[]{:S(2)}) copy-start(s32[4,1]{0,1:T(1,128)} %copy-done.6) | copy-start | bytes 52
  142.2 13.6 %collective-permute-start.4 = (bf16[512,768]{1,0:T(8,128)(2,1)}, bf16[512,768]{1,0:T(8,128)(2,1)S(1)}, u32[]{:S(2)}, u32[]{:S(2)}) collective-permute-start(bf16[512,768]{1,0:T(8,128)(2,1)} %shard_map.87), channel_id=1, source_target_pairs={{0,2},{2,0},{1,3},{3,1},{4,6},{6,4},{5,7},{7,5},{8,10},{10,8},{9,1... | collective-permute-start | bytes 2359304 | tf_op jit(solution)/shard_map/ppermute | solution.py:19
  144.6 19.8 %copy-start = (bf16[512,768]{1,0:T(8,128)(2,1)S(1)}, bf16[512,768]{1,0:T(8,128)(2,1)}, u32[]{:S(2)}) copy-start(bf16[512,768]{1,0:T(8,128)(2,1)} %shard_map.87) | copy-start | bytes 2359300
  157.8 10.5 %collective-permute-start.5 = (bf16[512,608]{0,1:T(8,128)(2,1)S(1)}, bf16[512,608]{0,1:T(8,128)(2,1)S(1)}, u32[]{:S(2)}, u32[]{:S(2)}) collective-permute-start(bf16[512,608]{0,1:T(8,128)(2,1)S(1)} %add_convert_fusion.1), channel_id=1, source_target_pairs={{0,1},{1,0},{2,3},{3,2},{4,5},{5,4},{6,7},{7,6},{8,9},{9,8},{10,11... | collective-permute-start | bytes 1867784 | tf_op jit(solution)/shard_map/ppermute | solution.py:19
